TPU v7x, 256 devices: a whole 4x4x8 slice. The times are simulated.
256 devices in a mesh: row: 32 (over z, y), col: 8 (over x, core).
Axes of the slice: x: 4, y: 4, z: 8, core: 2. Of those that a mesh axis runs over, the one named last changes fastest.
Arguments:
- amps: bfloat16 [30720, 30720], P(('col', 'row')), may hold values from -6 to 6
- cycle_int: bfloat16 [30720, 1024], P('col'), may hold values from -0.03125 to 0.03125
- tile_mask: int32 [480, 16], P('col'), may hold values 0 or 1
- coulomb: bfloat16 [30720, 1024], P('row', 'col'), may hold values from -6 to 6
- occ_irrep: int32 [240], replicated, may hold values from 0 to 7
- vir_irrep: int32 [192], replicated, may hold values from 0 to 7
- occ_energy: float32 [240], replicated, may hold values from -1.5 to -0.3
- vir_energy: float32 [192], replicated, may hold values from 0.3 to 2
Outputs:
- new_amps: bfloat16 [30720, 1024], P('row', 'col')
All inputs are finite; a program needn't handle non-finite values. No bound on the sum of `tile_mask` on one device may be relied on, other than what follows from the above.
Results may differ from a plain program's by a relative error of at most 0.001.
Values may be sent and summed in bfloat16 or wider, within the bound.
No kernel may reach another device: no remote copies, remote signals or barrier semaphores. Data moves between devices by JAX's collectives and lax.ppermute only.
A program may use at most 128 MiB of HBM per device.

v0:
```python
import jax
import jax.numpy as jnp
from jax import lax
from jax.sharding import Mesh, PartitionSpec as P

BLK = 64
Z, Y, X, C = ("z", "y", "x", "core")
COL = (X, C)
ROW = (Z, Y)


def lookup(positions, values_table):
    entries = jnp.arange(values_table.shape[0], dtype=jnp.int32)
    picked = jnp.where(
        positions[:, None] == entries[None, :],
        values_table[None, :],
        jnp.zeros((), values_table.dtype),
    )
    return jnp.sum(picked, axis=1)


def swap_perm(nz, nc):
    return [(z * nc + c, c * nz + z) for z in range(nz) for c in range(nc)]


def local(amps, cycle_int, tile_mask, coulomb, occ_irrep, vir_irrep, occ_energy, vir_energy):
    block_size = BLK
    occupied = occ_energy.shape[0]
    row_blocks = vir_energy.shape[0] // block_size - 1
    kc_rows, jb_all = cycle_int.shape
    rows_here, cols_here = coulomb.shape
    nz = lax.axis_size(Z)
    ny = lax.axis_size(Y)
    ncol = lax.axis_size(COL)
    z = lax.axis_index(Z)
    y = lax.axis_index(Y)
    c = lax.axis_index(COL)
    sub = amps.shape[0]
    span = sub * ny
    ci_rows = lax.dynamic_slice_in_dim(cycle_int, z * span, span, axis=0)
    mask_rows = jnp.repeat(tile_mask.astype(jnp.bfloat16), block_size, axis=0)
    mask_rows = lax.dynamic_slice_in_dim(mask_rows, z * span, span, axis=0)
    masked = (
        ci_rows.reshape(span, jb_all // block_size, block_size) * mask_rows[:, :, None]
    ).reshape(span, jb_all)
    masked_all = lax.all_gather(masked, COL, axis=0, tiled=True)
    plane_amps = lax.all_to_all(amps, (X, C, Y), split_axis=1, concat_axis=0, tiled=True)
    partial_value = lax.dot_general(
        plane_amps, masked_all, (((0,), (0,)), ((), ())), preferred_element_type=jnp.float32
    )
    cycle_sum = lax.psum_scatter(partial_value, Z, scatter_dimension=1, tiled=True)
    perm = swap_perm(nz, ncol)
    coulomb_here = lax.ppermute(coulomb, (Z, X, C), perm)
    row_block = c * ny + y
    row_pos = row_block * rows_here + jnp.arange(rows_here, dtype=jnp.int32)
    col_pos = z * cols_here + jnp.arange(cols_here, dtype=jnp.int32)
    occ_row = row_pos // block_size % occupied
    vir_row = block_size * (row_pos // (occupied * block_size)) + row_pos % block_size
    occ_col = col_pos // block_size % occupied
    vir_col = col_pos % block_size + row_blocks * block_size
    sym_row = jnp.bitwise_xor(lookup(occ_row, occ_irrep), lookup(vir_row, vir_irrep))
    sym_col = jnp.bitwise_xor(lookup(occ_col, occ_irrep), lookup(vir_col, vir_irrep))
    allowed = sym_row[:, None] == sym_col[None, :]
    gap_row = lookup(vir_row, vir_energy) - lookup(occ_row, occ_energy)
    gap_col = lookup(vir_col, vir_energy) - lookup(occ_col, occ_energy)
    denominator = gap_row[:, None] + gap_col[None, :]
    updated = (coulomb_here.astype(jnp.float32) + cycle_sum) / denominator
    out = jnp.where(allowed, updated, jnp.float32(0.0)).astype(jnp.bfloat16)
    return lax.ppermute(out, (Z, X, C), perm)


def solution(mesh):
    nrow, ncol = mesh.devices.shape
    ncore = 2
    nx = ncol // ncore
    nz = ncol
    ny = nrow // nz
    torus = Mesh(mesh.devices.reshape(nz, ny, nx, ncore), (Z, Y, X, C))
    return jax.shard_map(
        local,
        mesh=torus,
        in_specs=(P(COL + ROW, None), P(COL, None), P(COL, None), P(ROW, COL), P(), P(), P(), P()),
        out_specs=P(ROW, COL),
        check_vma=False,
    )
```

profile of v0, /device:TPU:7, one launch (start us, length us, event | category | flops | bytes accessed | tf_op | source)
XLA Modules:
  0.0 276.8 jit_solution(13097134514686713037)
XLA Ops:
  6.5 1.3 constant_dynamic-slice_fusion
  7.8 0.5 copy.22
  8.4 0.7 convert_element_type.10
  9.1 0.2 broadcast_in_dim.140
  9.3 0.3 reshape.119
  9.5 0.1 constant_dynamic-slice_fusion.1
  9.6 0.1 bitcast_multiply_fusion
  9.7 1.4 copy.19
  11.1 0.0 all-gather.2.cloned.1.call-update
  11.1 0.0 reduce-scatter.2.cloned.1.call-start
  11.1 10.1 %copy.20 = bf16[120,30720]{0,1:T(8,128)(2,1)} copy(bf16[120,30720]{1,0:T(8,128)(2,1)} %param.8) | data formatting | bytes 14745600 | tf_op args[0]
  21.3 126.3 %all_to_all.19 = bf16[120,32,960]{0,2,1:T(8,128)(2,1)S(1)} all-to-all(bf16[120,32,960]{0,2,1:T(8,128)(2,1)} %bitcast.13), channel_id=1, replica_groups=mesh['z'=8,'y'=4,'x'=4,'core'=2] {'x','core','y'}, dimensions={1} | all-to-all | bytes 14745600 | tf_op jit(solution)/shard_map/all_to_all | solution.py:47
  147.6 8.2 %copy.21 = bf16[32,120,960]{1,0,2:T(8,128)(2,1)} copy(bf16[32,120,960]{1,2,0:T(8,128)(2,1)S(1)} %bitcast.12) | data formatting | bytes 14745600 | tf_op jit(solution)/shard_map/all_to_all | solution.py:47
  155.8 15.6 %all_to_all.17 = bf16[3840,960]{0,1:T(8,128)(2,1)} reshape(bf16[32,120,960]{1,0,2:T(8,128)(2,1)} %copy.21) | data formatting | bytes 14745600 | tf_op jit(solution)/shard_map/all_to_all | solution.py:47
  171.5 0.0 all-gather.2.cloned.1.call-done
  171.5 13.7 %convolution_bitcast_fusion = f32[960,1024]{1,0:T(8,128)} fusion(bf16[3840,960]{0,1:T(8,128)(2,1)} %all_to_all.17, bf16[3840,1024]{1,0:T(8,128)(2,1)} %all-gather.2.cloned.1.call-done), kind=kOutput, calls=%fused_computation | convolution fusion | flops 7549747200 | bytes 19169280 | tf_op jit(solution)/shard_map/dot_general | solution.py:48
  185.2 0.0 reduce-scatter.2.cloned.1.call-update
  185.2 6.9 %collective-permute-start = (bf16[960,128]{1,0:T(8,128)(2,1)S(1)}, bf16[960,128]{1,0:T(8,128)(2,1)S(1)}, u32[]{:S(2)}, u32[]{:S(2)}) collective-permute-start(bf16[960,128]{1,0:T(8,128)(2,1)S(1)} %copy-done.4), channel_id=1, source_target_pairs={{0,0},{1,32},{2,64},{3,96},{4,128},{5,160},{6,192},{7,224},{32,1},... | collective-permute-start | bytes 737288 | tf_op jit(solution)/shard_map/ppermute | solution.py:53
  192.1 0.1 select_reduce_fusion.6
  192.2 0.1 select_reduce_fusion.4
  192.4 0.2 select_reduce_fusion.2
  192.6 0.4 select_reduce_fusion
  193.0 0.1 select_reduce_fusion.7
  193.1 0.1 select_reduce_fusion.5
  193.2 0.2 select_reduce_fusion.3
  193.4 0.4 select_reduce_fusion.1
  193.8 19.5 %collective-permute-done = bf16[960,128]{1,0:T(8,128)(2,1)S(1)} collective-permute-done((bf16[960,128]{1,0:T(8,128)(2,1)S(1)}, bf16[960,128]{1,0:T(8,128)(2,1)S(1)}, u32[]{:S(2)}, u32[]{:S(2)}) %collective-permute-start) | collective-permute-done | bytes 245792 | tf_op jit(solution)/shard_map/ppermute | solution.py:53
  213.3 33.6 %reduce-scatter.2.cloned.1.call-done = f32[960,128]{1,0:T(8,128)} async-done(((f32[960,1024]{1,0:T(8,128)}), f32[960,128]{1,0:T(8,128)}) %reduce-scatter.2.cloned.1.call-update) | async-done | bytes 491536 | tf_op jit(solution)/shard_map/reduce_scatter | solution.py:51
  246.8 1.3 select_convert_fusion
  248.2 3.0 %collective-permute-start.1 = (bf16[960,128]{1,0:T(8,128)(2,1)S(1)}, bf16[960,128]{1,0:T(8,128)(2,1)S(1)}, u32[]{:S(2)}, u32[]{:S(2)}) collective-permute-start(bf16[960,128]{1,0:T(8,128)(2,1)S(1)} %select_convert_fusion), channel_id=1, source_target_pairs={{0,0},{1,32},{2,64},{3,96},{4,128},{5,160},{6,192},{7,224},{32,1},... | collective-permute-start | bytes 737288 | tf_op jit(solution)/shard_map/ppermute | solution.py:69
  251.2 18.0 %collective-permute-done.1 = bf16[960,128]{1,0:T(8,128)(2,1)S(1)} collective-permute-done((bf16[960,128]{1,0:T(8,128)(2,1)S(1)}, bf16[960,128]{1,0:T(8,128)(2,1)S(1)}, u32[]{:S(2)}, u32[]{:S(2)}) %collective-permute-start.1) | collective-permute-done | bytes 245792 | tf_op jit(solution)/shard_map/ppermute | solution.py:69
  269.3 0.7 copy.24
  (17 shorter events, 0.1 us)
Async XLA Ops:
  6.5 164.9 %all-gather.2.cloned.1.call-start = ((), (), s32[]{:S(2)}) async-start(), calls=%async_computation.2 | async-start | bytes 8847360 | tf_op jit(solution)/shard_map/all_gather | solution.py:46
  11.1 235.7 %reduce-scatter.2.cloned.1.call-start = ((), (), s32[]{:S(2)}) async-start(), calls=%async_computation.3 | async-start | bytes 4423680 | tf_op jit(solution)/shard_map/reduce_scatter | solution.py:51
  171.4 13.8 %copy-start.4 = (bf16[960,128]{1,0:T(8,128)(2,1)S(1)}, bf16[960,128]{1,0:T(8,128)(2,1)}, u32[]{:S(2)}) copy-start(bf16[960,128]{1,0:T(8,128)(2,1)} %param.11) | copy-start | bytes 737284
  171.4 20.7 %copy-start = (f32[192]{0:T(256)S(1)}, f32[192]{0:T(256)}, u32[]{:S(2)}) copy-start(f32[192]{0:T(256)} %param.15) | copy-start | bytes 2308
  171.4 20.8 %copy-start.1 = (f32[240]{0:T(256)S(1)}, f32[240]{0:T(256)}, u32[]{:S(2)}) copy-start(f32[240]{0:T(256)} %param.14) | copy-start | bytes 2884
  171.4 21.5 %copy-start.2 = (s32[192]{0:T(256)S(1)}, s32[192]{0:T(256)}, u32[]{:S(2)}) copy-start(s32[192]{0:T(256)} %param.13) | copy-start | bytes 2308
  171.4 21.6 %copy-start.3 = (s32[240]{0:T(256)S(1)}, s32[240]{0:T(256)}, u32[]{:S(2)}) copy-start(s32[240]{0:T(256)} %param.12) | copy-start | bytes 2884
  185.2 28.1 %collective-permute-start = (bf16[960,128]{1,0:T(8,128)(2,1)S(1)}, bf16[960,128]{1,0:T(8,128)(2,1)S(1)}, u32[]{:S(2)}, u32[]{:S(2)}) collective-permute-start(bf16[960,128]{1,0:T(8,128)(2,1)S(1)} %copy-done.4), channel_id=1, source_target_pairs={{0,0},{1,32},{2,64},{3,96},{4,128},{5,160},{6,192},{7,224},{32,1},... | collective-permute-start | bytes 737288 | tf_op jit(solution)/shard_map/ppermute | solution.py:53
  248.2 21.1 %collective-permute-start.1 = (bf16[960,128]{1,0:T(8,128)(2,1)S(1)}, bf16[960,128]{1,0:T(8,128)(2,1)S(1)}, u32[]{:S(2)}, u32[]{:S(2)}) collective-permute-start(bf16[960,128]{1,0:T(8,128)(2,1)S(1)} %select_convert_fusion), channel_id=1, source_target_pairs={{0,0},{1,32},{2,64},{3,96},{4,128},{5,160},{6,192},{7,224},{32,1},... | collective-permute-start | bytes 737288 | tf_op jit(solution)/shard_map/ppermute | solution.py:69
Sparse Core Ops, SparseCore 0:
  11.2 113.2 all-gather.1
  185.3 61.4 reduce-scatter.1
where the time goes:
time: 278 us; the launch traced here: 277 us
  blocking collectives  126 us (45%)
  waiting for transfers between devices  71.2 us (26%)
  local copies, waits for them, and re-layouts  38.4 us (14%)
  matrix products  13.7 us (5%)
  between operations  13.6 us (5%)
  starting transfers between devices  9.94 us (4%)
  other arithmetic  3.68 us (1%)
    all_to_all x1, blocking collectives, local(): lax.all_to_all(amps, (X, C, Y), split_axis=1, concat_axis=0, tiled=True)  126 us
    reduce_scatter x1, waiting for transfers between devices, local(): lax.psum_scatter(partial_value, Z, scatter_dimension=1, tiled=True)  33.6 us
    all_to_all x2, local copies, waits for them, and re-layouts, local(): lax.all_to_all(amps, (X, C, Y), split_axis=1, concat_axis=0, tiled=True)  23.9 us
    ppermute x1, waiting for transfers between devices, local(): coulomb_here = lax.ppermute(coulomb, (Z, X, C), perm)  19.5 us
    ppermute x1, waiting for transfers between devices, local(): return lax.ppermute(out, (Z, X, C), perm)  18 us
    dot_general x1, matrix products, local(): lax.dot_general(plane_amps, masked_all, (((0,), (0,)), ((), ())), preferr...  13.7 us
    unnamed x13, local copies, waits for them, and re-layouts  11.4 us
    ppermute x1, starting transfers between devices, local(): coulomb_here = lax.ppermute(coulomb, (Z, X, C), perm)  6.88 us
  transfers between devices with their start and end apart: 4, of which 3 were waited for; matrix products, arithmetic and copies ran while one was open for 7% of the time, Pallas kernels for 0%

commit v1 on v0

--- a/solution.py
+++ b/solution.py
@@ -44,7 +44,11 @@
         ci_rows.reshape(span, jb_all // block_size, block_size) * mask_rows[:, :, None]
     ).reshape(span, jb_all)
     masked_all = lax.all_gather(masked, COL, axis=0, tiled=True)
-    plane_amps = lax.all_to_all(amps, (X, C, Y), split_axis=1, concat_axis=0, tiled=True)
+    ready = lax.axis_size((X, C, Y))
+    odd = jnp.split(amps, ready, axis=1)
+    w1 = jnp.stack(odd)
+    main = lax.all_to_all(w1, (X, C, Y), 0, 0)
+    plane_amps = jnp.concatenate(main, axis=0)
     partial_value = lax.dot_general(
         plane_amps, masked_all, (((0,), (0,)), ((), ())), preferred_element_type=jnp.float32
     )

time: 278 us -> 255 us (0.917)
  blocking collectives: 126 us -> 103 us
    all_to_all x2 -> x0, local copies, waits for them, and re-layouts: 23.9 us -> none  [local(): lax.all_to_all(amps, (X, C, Y), split_axis=1, concat_axis=0, tiled=True)]
    all_to_all x1, blocking collectives: 126 us -> 103 us  [local(): main = lax.all_to_all(w1, (X, C, Y), 0, 0)]
    unnamed x13 -> x43, local copies, waits for them, and re-layouts: 11.4 us -> 33.2 us
  transfers between devices with their start and end apart: 4 -> 4, of which waited for: 3 -> 3; matrix products, arithmetic and copies ran while one was open for 7% -> 14% of each run, Pallas kernels for 0% -> 0%
where the time goes in v1:
time: 255 us; the launch traced here: 253 us
  blocking collectives  103 us (40%)
  waiting for transfers between devices  71.3 us (28%)
  local copies, waits for them, and re-layouts  37.4 us (15%)
  matrix products  13.8 us (5%)
  between operations  13.8 us (5%)
  starting transfers between devices  10.2 us (4%)
  other arithmetic  3.68 us (1%)
    all_to_all x1, blocking collectives, local(): main = lax.all_to_all(w1, (X, C, Y), 0, 0)  103 us
    reduce_scatter x1, waiting for transfers between devices, local(): lax.psum_scatter(partial_value, Z, scatter_dimension=1, tiled=True)  33.4 us
    unnamed x43, local copies, waits for them, and re-layouts  33.2 us
    ppermute x1, waiting for transfers between devices, local(): coulomb_here = lax.ppermute(coulomb, (Z, X, C), perm)  19.5 us
    ppermute x1, waiting for transfers between devices, local(): return lax.ppermute(out, (Z, X, C), perm)  18.3 us
    dot_general x1, matrix products, local(): lax.dot_general(plane_amps, masked_all, (((0,), (0,)), ((), ())), preferr...  13.8 us
    ppermute x1, starting transfers between devices, local(): coulomb_here = lax.ppermute(coulomb, (Z, X, C), perm)  7.07 us
  transfers between devices with their start and end apart: 4, of which 3 were waited for; matrix products, arithmetic and copies ran while one was open for 14% of the time, Pallas kernels for 0%

profile of v1, /device:TPU:7, one launch (start us, length us, event | category | flops | bytes accessed | tf_op | source)
XLA Modules:
  0.0 253.4 jit_solution(12719601767798529318)
XLA Ops:
  6.5 1.3 constant_dynamic-slice_fusion
  9.7 1.3 copy.15
  12.1 1.1 bitcast_dynamic-update-slice_fusion.30
  13.2 1.0 bitcast_dynamic-update-slice_fusion.29
  14.1 1.1 bitcast_dynamic-update-slice_fusion.28
  16.2 1.1 bitcast_dynamic-update-slice_fusion.26
  18.2 1.1 bitcast_dynamic-update-slice_fusion.24
  20.3 1.1 bitcast_dynamic-update-slice_fusion.22
  22.4 1.1 bitcast_dynamic-update-slice_fusion.20
  24.4 1.1 bitcast_dynamic-update-slice_fusion.18
  25.5 1.0 bitcast_dynamic-update-slice_fusion.17
  26.5 1.1 bitcast_dynamic-update-slice_fusion.16
  27.7 1.0 bitcast_dynamic-update-slice_fusion.15
  28.7 1.1 bitcast_dynamic-update-slice_fusion.14
  30.7 1.1 bitcast_dynamic-update-slice_fusion.12
  31.8 1.0 bitcast_dynamic-update-slice_fusion.11
  32.8 1.1 bitcast_dynamic-update-slice_fusion.10
  34.9 1.1 bitcast_dynamic-update-slice_fusion.8
  37.0 1.1 bitcast_dynamic-update-slice_fusion.6
  38.1 1.0 bitcast_dynamic-update-slice_fusion.5
  39.1 1.1 bitcast_dynamic-update-slice_fusion.4
  40.2 1.0 bitcast_dynamic-update-slice_fusion.3
  41.1 1.1 bitcast_dynamic-update-slice_fusion.2
  43.2 1.1 bitcast_dynamic-update-slice_fusion
  44.3 103.3 %all_to_all.5 = bf16[32,120,960]{2,1,0:T(8,128)(2,1)} all-to-all(bf16[32,120,960]{2,1,0:T(8,128)(2,1)S(1)} %bitcast_dynamic-update-slice_fusion), channel_id=1, replica_groups=mesh['z'=8,'y'=4,'x'=4,'core'=2] {'x','core','y'}, dimensions={0} | all-to-all | bytes 14745600 | tf_op jit(solution)/shard_map/all_to_all | solution.py:50
  147.6 13.8 %fusion.9 = f32[960,1024]{1,0:T(8,128)} fusion(bf16[3840,960]{1,0:T(8,128)(2,1)} %bitcast.71, bf16[3840,1024]{1,0:T(8,128)(2,1)} %all-gather.2.cloned.1.call-done), kind=kOutput, calls=%fused_computation.74 | convolution fusion | flops 7549747200 | bytes 19169280 | tf_op jit(solution)/shard_map/dot_general | solution.py:52
  161.5 7.1 %collective-permute-start = (bf16[960,128]{1,0:T(8,128)(2,1)S(1)}, bf16[960,128]{1,0:T(8,128)(2,1)S(1)}, u32[]{:S(2)}, u32[]{:S(2)}) collective-permute-start(bf16[960,128]{1,0:T(8,128)(2,1)S(1)} %copy-done.4), channel_id=1, source_target_pairs={{0,0},{1,32},{2,64},{3,96},{4,128},{5,160},{6,192},{7,224},{32,1},... | collective-permute-start | bytes 737288 | tf_op jit(solution)/shard_map/ppermute | solution.py:57
  170.2 19.5 %collective-permute-done = bf16[960,128]{1,0:T(8,128)(2,1)S(1)} collective-permute-done((bf16[960,128]{1,0:T(8,128)(2,1)S(1)}, bf16[960,128]{1,0:T(8,128)(2,1)S(1)}, u32[]{:S(2)}, u32[]{:S(2)}) %collective-permute-start) | collective-permute-done | bytes 245792 | tf_op jit(solution)/shard_map/ppermute | solution.py:57
  189.7 33.4 %reduce-scatter.2.cloned.1.call-done = f32[960,128]{1,0:T(8,128)} async-done(((f32[960,1024]{1,0:T(8,128)}), f32[960,128]{1,0:T(8,128)}) %reduce-scatter.2.cloned.1.call-update) | async-done | bytes 491536 | tf_op jit(solution)/shard_map/reduce_scatter | solution.py:55
  223.2 1.3 select_convert_fusion
  224.5 3.0 %collective-permute-start.1 = (bf16[960,128]{1,0:T(8,128)(2,1)S(1)}, bf16[960,128]{1,0:T(8,128)(2,1)S(1)}, u32[]{:S(2)}, u32[]{:S(2)}) collective-permute-start(bf16[960,128]{1,0:T(8,128)(2,1)S(1)} %select_convert_fusion), channel_id=1, source_target_pairs={{0,0},{1,32},{2,64},{3,96},{4,128},{5,160},{6,192},{7,224},{32,1},... | collective-permute-start | bytes 737288 | tf_op jit(solution)/shard_map/ppermute | solution.py:73
  227.6 18.3 %collective-permute-done.1 = bf16[960,128]{1,0:T(8,128)(2,1)S(1)} collective-permute-done((bf16[960,128]{1,0:T(8,128)(2,1)S(1)}, bf16[960,128]{1,0:T(8,128)(2,1)S(1)}, u32[]{:S(2)}, u32[]{:S(2)}) %collective-permute-start.1) | collective-permute-done | bytes 245792 | tf_op jit(solution)/shard_map/ppermute | solution.py:73
  (46 shorter events, 13.9 us)
Async XLA Ops:
  6.5 141.1 %all-gather.2.cloned.1.call-start = ((), (), s32[]{:S(2)}) async-start(), calls=%async_computation.2 | async-start | bytes 8847360 | tf_op jit(solution)/shard_map/all_gather | solution.py:46
  11.0 212.1 %reduce-scatter.2.cloned.1.call-start = ((), (), s32[]{:S(2)}) async-start(), calls=%async_computation.3 | async-start | bytes 4423680 | tf_op jit(solution)/shard_map/reduce_scatter | solution.py:55
  147.6 13.8 %copy-start.4 = (bf16[960,128]{1,0:T(8,128)(2,1)S(1)}, bf16[960,128]{1,0:T(8,128)(2,1)}, u32[]{:S(2)}) copy-start(bf16[960,128]{1,0:T(8,128)(2,1)} %param.11) | copy-start | bytes 737284
  147.6 21.0 %copy-start = (f32[192]{0:T(256)S(1)}, f32[192]{0:T(256)}, u32[]{:S(2)}) copy-start(f32[192]{0:T(256)} %param.15) | copy-start | bytes 2308
  147.6 21.1 %copy-start.1 = (f32[240]{0:T(256)S(1)}, f32[240]{0:T(256)}, u32[]{:S(2)}) copy-start(f32[240]{0:T(256)} %param.14) | copy-start | bytes 2884
  147.6 21.8 %copy-start.2 = (s32[192]{0:T(256)S(1)}, s32[192]{0:T(256)}, u32[]{:S(2)}) copy-start(s32[192]{0:T(256)} %param.13) | copy-start | bytes 2308
  147.6 21.9 %copy-start.3 = (s32[240]{0:T(256)S(1)}, s32[240]{0:T(256)}, u32[]{:S(2)}) copy-start(s32[240]{0:T(256)} %param.12) | copy-start | bytes 2884
  161.5 28.3 %collective-permute-start = (bf16[960,128]{1,0:T(8,128)(2,1)S(1)}, bf16[960,128]{1,0:T(8,128)(2,1)S(1)}, u32[]{:S(2)}, u32[]{:S(2)}) collective-permute-start(bf16[960,128]{1,0:T(8,128)(2,1)S(1)} %copy-done.4), channel_id=1, source_target_pairs={{0,0},{1,32},{2,64},{3,96},{4,128},{5,160},{6,192},{7,224},{32,1},... | collective-permute-start | bytes 737288 | tf_op jit(solution)/shard_map/ppermute | solution.py:57
  224.5 21.4 %collective-permute-start.1 = (bf16[960,128]{1,0:T(8,128)(2,1)S(1)}, bf16[960,128]{1,0:T(8,128)(2,1)S(1)}, u32[]{:S(2)}, u32[]{:S(2)}) collective-permute-start(bf16[960,128]{1,0:T(8,128)(2,1)S(1)} %select_convert_fusion), channel_id=1, source_target_pairs={{0,0},{1,32},{2,64},{3,96},{4,128},{5,160},{6,192},{7,224},{32,1},... | collective-permute-start | bytes 737288 | tf_op jit(solution)/shard_map/ppermute | solution.py:73
Sparse Core Ops, SparseCore 0:
  11.2 66.0 all-gather.1
  161.6 61.5 reduce-scatter.1
